TPU v7x, 512 devices: a whole 4x8x8 slice. The times are simulated.
512 devices in a mesh: wide: 64 (over y, z), narrow: 8 (over x, core).
Axes of the slice: x: 4, y: 8, z: 8, core: 2. Of those that a mesh axis runs over, the one named last changes fastest.
Arguments:
- amplitudes: bfloat16 [384, 2048], P('wide', 'narrow'), may hold values from -6 to 6
- integrals: bfloat16 [262144, 2048], P('wide', 'narrow'), may hold values from -0.375 to 0.375
- virtual_irrep: int32 [512], replicated, may hold values from 0 to 7
- column_irrep: int32 [2048], P('narrow'), may hold values from 0 to 7
- pair_energy: float32 [384], P('narrow'), may hold values from -4 to -1
- virtual_energy: float32 [512], replicated, may hold values from 0.5 to 3
- residual_in: bfloat16 [384, 262144], P('narrow', 'wide'), may hold values from -6 to 6
Outputs:
- new_amplitudes: bfloat16 [384, 262144], P('narrow', 'wide')
All inputs are finite; a program needn't handle non-finite values.
Results may differ from a plain program's by a relative error of at most 0.012.
Values may be sent and summed in bfloat16 or wider, within the bound.
No kernel may reach another device: no remote copies, remote signals or barrier semaphores. Data moves between devices by JAX's collectives and lax.ppermute only.
A program may use at most 64 MiB of HBM per device.

v0:
```python
import jax
import jax.numpy as jnp
from jax import lax
from jax.sharding import PartitionSpec as P


def local(
    amplitudes, integrals, virtual_irrep, column_irrep, pair_energy, virtual_energy, residual_in
):
    wide_size = lax.axis_size("wide")
    num_virt = virtual_irrep.shape[0]
    a_local = num_virt // wide_size
    first_a = lax.axis_index("wide") * a_local
    local_irrep = lax.dynamic_slice_in_dim(virtual_irrep, first_a, a_local, 0)
    row_irrep = jnp.bitwise_xor(local_irrep[:, None], virtual_irrep[None, :]).reshape(
        a_local * num_virt
    )
    masked = jnp.where(
        row_irrep[:, None] == column_irrep[None, :], integrals, jnp.zeros((), integrals.dtype)
    )
    contract = (((1,), (1,)), ((), ()))
    terms = lax.dot_general(
        lax.all_gather(amplitudes, "wide", axis=0, tiled=True),
        masked,
        contract,
        preferred_element_type=jnp.float32,
    )
    ladder = lax.psum_scatter(
        terms.astype(jnp.bfloat16), "narrow", scatter_dimension=0, tiled=True
    ).astype(jnp.float32)
    pair_rows = ladder.shape[0]
    ladder_cube = ladder.reshape(pair_rows, a_local, num_virt)
    swapped = lax.all_to_all(
        ladder_cube.astype(jnp.bfloat16), "wide", split_axis=2, concat_axis=2, tiled=True
    ).astype(ladder_cube.dtype)
    mirrored = swapped.reshape(pair_rows, a_local, wide_size, a_local)
    mirrored = jnp.transpose(mirrored, (0, 3, 2, 1)).reshape(pair_rows, a_local * num_virt)
    local_energy = lax.dynamic_slice_in_dim(virtual_energy, first_a, a_local, 0)
    denominator = (
        pair_energy[:, None, None] - local_energy[None, :, None] - virtual_energy[None, None, :]
    )
    denominator = denominator.reshape(pair_rows, a_local * num_virt)
    total = residual_in.astype(jnp.float32) + ladder - mirrored
    return (total / denominator).astype(jnp.bfloat16)


def solution(mesh):
    return jax.shard_map(
        local,
        mesh=mesh,
        in_specs=(
            P("wide", "narrow"),
            P("wide", "narrow"),
            P(),
            P("narrow"),
            P("narrow"),
            P(),
            P("narrow", "wide"),
        ),
        out_specs=P("narrow", "wide"),
        check_vma=False,
    )
```

profile of v0, /device:TPU:23, one launch (start us, length us, event | category | flops | bytes accessed | tf_op | source)
XLA Modules:
  0.0 151.3 jit_solution(6612598673634443218)
XLA Ops:
  6.5 0.0 reduce-scatter.4.cloned.1.call-start
  6.5 0.8 dynamic_slice.6
  7.3 0.8 xor_bitcast_fusion
  8.1 44.1 %all-gather = bf16[64,6,256]{2,1,0:T(8,128)(2,1)S(1)} all-gather(bf16[1,6,256]{2,1,0:T(8,128)(2,1)} %bitcast.31), channel_id=1, replica_groups=mesh['wide'=64,'narrow'=8] {'wide'}, dimensions={0}, use_global_device_ids=true | all-gather | bytes 199680 | tf_op jit(solution)/shard_map/all_gather | solution.py:23
  52.1 0.1 reshape.74
  52.2 2.8 %fusion = bf16[384,4096]{0,1:T(8,128)(2,1)S(1)} fusion(bf16[384,256]{1,0:T(8,128)(2,1)S(1)} %reshape.74, bf16[4096,256]{1,0:T(8,128)(2,1)} %param.8, s32[256]{0:T(256)} %param.10, s32[4096]{0:T(1024)S(1)} %bitcast.30), kind=kOutput, calls=%fused_computation.1 | convolution fusion | flops 808976384 | bytes 5456896 | tf_op jit(solution)/shard_map/dot_general | solution.py:22
  55.0 2.9 %copy.25 = bf16[384,4096]{1,0:T(8,128)(2,1)} copy(bf16[384,4096]{0,1:T(8,128)(2,1)S(1)} %fusion) | data formatting | bytes 6291456
  57.9 0.0 reduce-scatter.4.cloned.1.call-update
  57.9 47.4 %reduce-scatter.4.cloned.1.call-done = bf16[48,4096]{1,0:T(8,128)(2,1)} async-done(((bf16[384,4096]{1,0:T(8,128)(2,1)}), bf16[48,4096]{1,0:T(8,128)(2,1)}) %reduce-scatter.4.cloned.1.call-update) | async-done | bytes 393232 | tf_op jit(solution)/shard_map/reduce_scatter | solution.py:28
  105.4 1.5 copy.26
  106.8 0.0 copy-start.2
  106.8 0.0 copy-start.3
  106.9 0.7 copy.31
  107.5 2.5 %reshape.77 = bf16[64,2,1536]{2,1,0:T(2,128)(2,1)} reshape(bf16[512,8,48]{2,1,0:T(8,128)(2,1)S(1)} %bitcast.25) | data formatting | bytes 786432
  110.0 12.8 %all-to-all-start = ((bf16[64,2,1536]{2,1,0:T(2,128)(2,1)}), bf16[64,2,1536]{2,1,0:T(2,128)(2,1)S(1)}, u32[]{:S(2)}, u32[]{:S(2)}) async-start(bf16[64,2,1536]{2,1,0:T(2,128)(2,1)} %reshape.77), calls=%async_computation | async-start | bytes 786432 | tf_op jit(solution)/shard_map/all_to_all | solution.py:33
  122.8 0.0 copy-done.2
  122.9 0.1 dynamic_slice.7
  122.9 0.0 copy-done.3
  122.9 0.1 broadcast_subtract_fusion
  123.0 0.1 sub.45
  123.1 1.3 copy.28
  124.5 15.1 %all-to-all-done = bf16[64,2,1536]{2,1,0:T(2,128)(2,1)S(1)} async-done(((bf16[64,2,1536]{2,1,0:T(2,128)(2,1)}), bf16[64,2,1536]{2,1,0:T(2,128)(2,1)S(1)}, u32[]{:S(2)}, u32[]{:S(2)}) %all-to-all-start) | async-done | bytes 393248 | tf_op jit(solution)/shard_map/all_to_all | solution.py:33
  139.6 1.0 reshape.78
  140.6 0.1 copy.23
  140.8 0.0 copy-start
  140.8 0.0 copy-start.1
  140.8 1.5 copy.24
  142.3 0.0 copy-done
  142.3 0.0 copy-done.1
  142.3 2.2 %divide_convert_fusion = bf16[48,4096]{1,0:T(8,128)(2,1)} fusion(f32[48,4096]{1,0:T(8,128)S(1)} %bitcast.28, f32[48,4096]{1,0:T(8,128)} %copy.24, bf16[48,4096]{1,0:T(8,128)(2,1)S(1)} %copy-done.1, bf16[48,4096]{1,0:T(8,128)(2,1)} %param.13, f32[4096]{0:T(1024)S(1)} %bitcast.29), kind=kLoop, calls=%fused_computation.6 | loop fusion | flops 1376256 | bytes 2768896 | tf_op jit(solution)/shard_map/convert_element_type | solution.py:44
  (3 shorter events, 0.0 us)
Async XLA Ops:
  6.5 98.8 %reduce-scatter.4.cloned.1.call-start = ((), (), s32[]{:S(2)}) async-start(), calls=%async_computation.2 | async-start | bytes 3538944 | tf_op jit(solution)/shard_map/reduce_scatter | solution.py:28
  106.8 16.0 %copy-start.2 = (f32[512]{0:T(512)S(1)}, f32[512]{0:T(512)}, u32[]{:S(2)}) copy-start(f32[512]{0:T(512)} %param.12) | copy-start | bytes 6148
  106.8 16.1 %copy-start.3 = (f32[48]{0:T(128)S(1)}, f32[48]{0:T(128)}, u32[]{:S(2)}) copy-start(f32[48]{0:T(128)} %param.11) | copy-start | bytes 580
  110.0 29.6 %all-to-all-start = ((bf16[64,2,1536]{2,1,0:T(2,128)(2,1)}), bf16[64,2,1536]{2,1,0:T(2,128)(2,1)S(1)}, u32[]{:S(2)}, u32[]{:S(2)}) async-start(bf16[64,2,1536]{2,1,0:T(2,128)(2,1)} %reshape.77), calls=%async_computation | async-start | bytes 786432 | tf_op jit(solution)/shard_map/all_to_all | solution.py:33
  140.8 1.5 copy-start
  140.8 1.5 copy-start.1
Sparse Core Ops, SparseCore 0:
  58.1 47.2 reduce-scatter.3
where the time goes:
time: 152 us; the launch traced here: 151 us
  waiting for transfers between devices  62.5 us (41%)
  blocking collectives  44.1 us (29%)
  between operations  13.5 us (9%)
  starting transfers between devices  12.8 us (8%)
  local copies, waits for them, and re-layouts  12.6 us (8%)
  other arithmetic  3 us (2%)
  matrix products  2.8 us (2%)
    reduce_scatter x1, waiting for transfers between devices, local(): lax.psum_scatter(terms.astype(jnp.bfloat16), 'narrow', scatter_dimension=...  47.4 us
    all_gather x1, blocking collectives, local(): lax.all_gather(amplitudes, 'wide', axis=0, tiled=True)  44.1 us
    all_to_all x1, waiting for transfers between devices, local(): lax.all_to_all(ladder_cube.astype(jnp.bfloat16), 'wide', split_axis=2, co...  15.1 us
    all_to_all x1, starting transfers between devices, local(): lax.all_to_all(ladder_cube.astype(jnp.bfloat16), 'wide', split_axis=2, co...  12.8 us
    unnamed x17, local copies, waits for them, and re-layouts  9.39 us
  transfers between devices with their start and end apart: 2, of which 2 were waited for; matrix products, arithmetic and copies ran while one was open for 1% of the time, Pallas kernels for 0%

commit v1 on v0

--- a/solution.py
+++ b/solution.py
@@ -20,7 +20,9 @@
     )
     contract = (((1,), (1,)), ((), ()))
     terms = lax.dot_general(
-        lax.all_gather(amplitudes, "wide", axis=0, tiled=True),
+        jnp.concatenate(
+            lax.all_to_all(jnp.stack([amplitudes] * lax.axis_size("wide")), "wide", 0, 0), axis=0
+        ),
         masked,
         contract,
         preferred_element_type=jnp.float32,

time: 152 us -> 123 us (0.81)
  blocking collectives: 44.1 us -> 0 us
  starting transfers between devices: 12.8 us -> 28.8 us
  waiting for transfers between devices: 62.5 us -> 60.6 us
    all_gather x1 -> x0, blocking collectives: 44.1 us -> none  [local(): lax.all_gather(amplitudes, 'wide', axis=0, tiled=True)]
    all_to_all x0 -> x1, starting transfers between devices: none -> 15.9 us  [local(): lax.all_to_all(jnp.stack([amplitudes] * lax.axis_size('wide')), 'wide', 0...]
    reduce_scatter x1, waiting for transfers between devices: 47.4 us -> 33.9 us  [local(): lax.psum_scatter(terms.astype(jnp.bfloat16), 'narrow', scatter_dimension=...]
    all_to_all x0 -> x1, waiting for transfers between devices: none -> 11.6 us  [local(): lax.all_to_all(jnp.stack([amplitudes] * lax.axis_size('wide')), 'wide', 0...]
    unnamed x17 -> x16, local copies, waits for them, and re-layouts: 9.39 us -> 9.33 us
  transfers between devices with their start and end apart: 2 -> 3, of which waited for: 2 -> 3; matrix products, arithmetic and copies ran while one was open for 1% -> 3% of each run, Pallas kernels for 0% -> 0%
where the time goes in v1:
time: 123 us
  waiting for transfers between devices  60.6 us (49%)
  starting transfers between devices  28.8 us (23%)
  local copies, waits for them, and re-layouts  14 us (11%)
  between operations  13.5 us (11%)
  other arithmetic  3 us (2%)
  matrix products  2.79 us (2%)
    reduce_scatter x1, waiting for transfers between devices, local(): lax.psum_scatter(terms.astype(jnp.bfloat16), 'narrow', scatter_dimension=...  33.9 us
    all_to_all x1, starting transfers between devices, local(): lax.all_to_all(jnp.stack([amplitudes] * lax.axis_size('wide')), 'wide', 0...  15.9 us
    all_to_all x1, waiting for transfers between devices, local(): lax.all_to_all(ladder_cube.astype(jnp.bfloat16), 'wide', split_axis=2, co...  15.1 us
    all_to_all x1, starting transfers between devices, local(): lax.all_to_all(ladder_cube.astype(jnp.bfloat16), 'wide', split_axis=2, co...  12.8 us
    all_to_all x1, waiting for transfers between devices, local(): lax.all_to_all(jnp.stack([amplitudes] * lax.axis_size('wide')), 'wide', 0...  11.6 us
    unnamed x16, local copies, waits for them, and re-layouts  9.33 us
    dot_general x1, matrix products, local(): lax.dot_general(jnp.concatenate(lax.all_to_all(jnp.stack([amplitudes] * l...  2.79 us
  transfers between devices with their start and end apart: 3, of which 3 were waited for; matrix products, arithmetic and copies ran while one was open for 3% of the time, Pallas kernels for 0%

profile of v1, /device:TPU:23, one launch (start us, length us, event | category | flops | bytes accessed | tf_op | source)
XLA Modules:
  0.0 122.7 jit_solution(12665315649769780214)
XLA Ops:
  6.5 1.4 %stack.2 = bf16[64,6,256]{2,1,0:T(8,128)(2,1)} broadcast(bf16[6,256]{1,0:T(8,128)(2,1)} %param.7), dimensions={1,2} | broadcast | bytes 199680 | tf_op jit(solution)/shard_map/stack | solution.py:24
  7.9 15.9 %all-to-all-start = ((bf16[64,6,256]{2,1,0:T(8,128)(2,1)}), bf16[64,6,256]{2,1,0:T(8,128)(2,1)S(1)}, u32[]{:S(2)}, u32[]{:S(2)}) async-start(bf16[64,6,256]{2,1,0:T(8,128)(2,1)} %stack.2), calls=%async_computation | async-start | bytes 524288 | tf_op jit(solution)/shard_map/all_to_all | solution.py:24
  23.9 0.0 reduce-scatter.4.cloned.1.call-start
  23.9 0.8 dynamic_slice.6
  24.7 0.8 xor_bitcast_fusion
  25.4 11.6 %all-to-all-done = bf16[64,6,256]{2,1,0:T(8,128)(2,1)S(1)} async-done(((bf16[64,6,256]{2,1,0:T(8,128)(2,1)}), bf16[64,6,256]{2,1,0:T(8,128)(2,1)S(1)}, u32[]{:S(2)}, u32[]{:S(2)}) %all-to-all-start) | async-done | bytes 196640 | tf_op jit(solution)/shard_map/all_to_all | solution.py:24
  37.0 0.1 reshape.70
  37.1 2.8 %fusion = bf16[384,4096]{0,1:T(8,128)(2,1)S(1)} fusion(bf16[384,256]{1,0:T(8,128)(2,1)S(1)} %reshape.70, bf16[4096,256]{1,0:T(8,128)(2,1)} %param.8, s32[256]{0:T(256)} %param.10, s32[4096]{0:T(1024)S(1)} %bitcast.29), kind=kOutput, calls=%fused_computation.1 | convolution fusion | flops 808976384 | bytes 5456896 | tf_op jit(solution)/shard_map/dot_general | solution.py:22
  39.9 2.9 %copy.25 = bf16[384,4096]{1,0:T(8,128)(2,1)} copy(bf16[384,4096]{0,1:T(8,128)(2,1)S(1)} %fusion) | data formatting | bytes 6291456
  42.8 0.0 reduce-scatter.4.cloned.1.call-update
  42.8 33.9 %reduce-scatter.4.cloned.1.call-done = bf16[48,4096]{1,0:T(8,128)(2,1)} async-done(((bf16[384,4096]{1,0:T(8,128)(2,1)}), bf16[48,4096]{1,0:T(8,128)(2,1)}) %reduce-scatter.4.cloned.1.call-update) | async-done | bytes 393232 | tf_op jit(solution)/shard_map/reduce_scatter | solution.py:30
  76.8 1.5 %copy.26 = bf16[48,4096]{0,1:T(8,128)(2,1)S(1)} copy(bf16[48,4096]{1,0:T(8,128)(2,1)} %reduce-scatter.4.cloned.1.call-done) | data formatting | bytes 786432
  78.2 0.0 copy-start.2
  78.3 0.0 copy-start.3
  78.3 0.7 copy.31
  79.0 2.5 %reshape.81 = bf16[64,2,1536]{2,1,0:T(2,128)(2,1)} reshape(bf16[512,8,48]{2,1,0:T(8,128)(2,1)S(1)} %bitcast.24) | data formatting | bytes 786432
  81.4 12.8 %all-to-all-start.1 = ((bf16[64,2,1536]{2,1,0:T(2,128)(2,1)}), bf16[64,2,1536]{2,1,0:T(2,128)(2,1)S(1)}, u32[]{:S(2)}, u32[]{:S(2)}) async-start(bf16[64,2,1536]{2,1,0:T(2,128)(2,1)} %reshape.81), calls=%async_computation.1 | async-start | bytes 786432 | tf_op jit(solution)/shard_map/all_to_all | solution.py:35
  94.2 0.0 copy-done.2
  94.3 0.1 dynamic_slice.7
  94.3 0.0 copy-done.3
  94.3 0.1 broadcast_subtract_fusion
  94.4 0.1 sub.45
  94.5 1.4 %copy.28 = f32[6,8,8,512]{3,1,2,0:T(8,128)} copy(f32[6,8,8,512]{3,2,1,0:T(8,128)S(1)} %bitcast.26) | data formatting | bytes 1572864
  95.9 15.1 %all-to-all-done.1 = bf16[64,2,1536]{2,1,0:T(2,128)(2,1)S(1)} async-done(((bf16[64,2,1536]{2,1,0:T(2,128)(2,1)}), bf16[64,2,1536]{2,1,0:T(2,128)(2,1)S(1)}, u32[]{:S(2)}, u32[]{:S(2)}) %all-to-all-start.1) | async-done | bytes 393248 | tf_op jit(solution)/shard_map/all_to_all | solution.py:35
  111.0 1.0 reshape.82
  112.1 0.1 copy.23
  112.2 0.0 copy-start
  112.2 0.0 copy-start.1
  112.2 1.5 %copy.24 = f32[48,4096]{1,0:T(8,128)} copy(f32[48,4096]{0,1:T(8,128)S(1)} %bitcast.22) | data formatting | bytes 1572864 | tf_op jit(solution)/shard_map/reshape | solution.py:39
  113.7 0.0 copy-done
  113.7 0.0 copy-done.1
  113.7 2.2 %divide_convert_fusion = bf16[48,4096]{1,0:T(8,128)(2,1)} fusion(f32[48,4096]{1,0:T(8,128)S(1)} %bitcast.27, f32[48,4096]{1,0:T(8,128)} %copy.24, bf16[48,4096]{1,0:T(8,128)(2,1)S(1)} %copy-done.1, bf16[48,4096]{1,0:T(8,128)(2,1)} %param.13, f32[4096]{0:T(1024)S(1)} %bitcast.28), kind=kLoop, calls=%fused_computation.6 | loop fusion | flops 1376256 | bytes 2768896 | tf_op jit(solution)/shard_map/convert_element_type | solution.py:46
  (3 shorter events, 0.0 us)
Async XLA Ops:
  7.9 29.1 %all-to-all-start = ((bf16[64,6,256]{2,1,0:T(8,128)(2,1)}), bf16[64,6,256]{2,1,0:T(8,128)(2,1)S(1)}, u32[]{:S(2)}, u32[]{:S(2)}) async-start(bf16[64,6,256]{2,1,0:T(8,128)(2,1)} %stack.2), calls=%async_computation | async-start | bytes 524288 | tf_op jit(solution)/shard_map/all_to_all | solution.py:24
  23.9 52.9 %reduce-scatter.4.cloned.1.call-start = ((), (), s32[]{:S(2)}) async-start(), calls=%async_computation.3 | async-start | bytes 3538944 | tf_op jit(solution)/shard_map/reduce_scatter | solution.py:30
  78.2 16.0 %copy-start.2 = (f32[512]{0:T(512)S(1)}, f32[512]{0:T(512)}, u32[]{:S(2)}) copy-start(f32[512]{0:T(512)} %param.12) | copy-start | bytes 6148
  78.3 16.1 %copy-start.3 = (f32[48]{0:T(128)S(1)}, f32[48]{0:T(128)}, u32[]{:S(2)}) copy-start(f32[48]{0:T(128)} %param.11) | copy-start | bytes 580
  81.4 29.6 %all-to-all-start.1 = ((bf16[64,2,1536]{2,1,0:T(2,128)(2,1)}), bf16[64,2,1536]{2,1,0:T(2,128)(2,1)S(1)}, u32[]{:S(2)}, u32[]{:S(2)}) async-start(bf16[64,2,1536]{2,1,0:T(2,128)(2,1)} %reshape.81), calls=%async_computation.1 | async-start | bytes 786432 | tf_op jit(solution)/shard_map/all_to_all | solution.py:35
  112.2 1.5 %copy-start = (f32[6,8,8,512]{3,1,2,0:T(8,128)S(1)}, f32[6,8,8,512]{3,1,2,0:T(8,128)}, u32[]{:S(2)}) copy-start(f32[6,8,8,512]{3,1,2,0:T(8,128)} %copy.28) | copy-start | bytes 2359300
  112.2 1.5 %copy-start.1 = (bf16[48,4096]{1,0:T(8,128)(2,1)S(1)}, bf16[48,4096]{1,0:T(8,128)(2,1)}, u32[]{:S(2)}) copy-start(bf16[48,4096]{1,0:T(8,128)(2,1)} %reduce-scatter.4.cloned.1.call-done) | copy-start | bytes 1179652
Sparse Core Ops, SparseCore 0:
  43.0 33.7 reduce-scatter.3
